TPU v7x, 32 devices: a whole 2x2x4 slice. The times are simulated.
32 devices in a mesh: leaf: 8 (over z, y), panel: 4 (over x, core).
Axes of the slice: x: 2, y: 2, z: 4, core: 2. Of those that a mesh axis runs over, the one named last changes fastest.
Arguments:
- interface_block: float32 [8, 2048, 2048], P('leaf', 'panel'), may hold values from -0.125 to 0.125
- coupling: bfloat16 [8, 2048, 128], P('leaf', 'panel'), may hold values from -0.375 to 0.375
- eigenvalues: float32 [8, 128], P('leaf'), may hold values from 0.5 to 8
- mode_counts: int32 [8], P('leaf'), may hold values from 64 to 128, as said below
- interface_coords: bfloat16 [8, 2048, 1024], P('leaf', 'panel'), may hold values from -6 to 6
- modal_coords: bfloat16 [8, 128, 4096], P('leaf'), may hold values from -6 to 6
Outputs:
- mode_shapes: float32 [8, 2048, 1024], P('leaf', 'panel')
Inputs may be any that keep to these rules, and one draw needn't show every extreme that they name: `mode_counts`: modes kept by each substructure; some substructure keeps all 128.
All inputs are finite; a program needn't handle non-finite values.
Results may differ from a plain program's by a relative error of at most 0.0023.
Values may be sent and summed in bfloat16 or wider, within the bound.
No kernel may reach another device: no remote copies, remote signals or barrier semaphores. Data moves between devices by JAX's collectives and lax.ppermute only.
A program may use at most 128 MiB of HBM per device.

v0:
```python
import jax
import jax.numpy as jnp
from jax import lax
from jax.sharding import PartitionSpec as P

LEVELS = 2


def partner(value, axis, bit):
    return lax.ppermute(value, axis, [(i, i ^ 1 << bit) for i in range(lax.axis_size(axis))])


def modal_reduce(summed, levels):
    leaf_index = lax.axis_index("leaf")
    current = summed
    for level in range(levels - 1, -1, -1):
        half = current.shape[1] // 2
        my_bit = leaf_index >> level & 1
        keep = lax.dynamic_slice_in_dim(current, my_bit * half, half, 1)
        other = lax.dynamic_slice_in_dim(current, (1 - my_bit) * half, half, 1)
        current = keep + partner(other, "leaf", level)
    return current


def on_device(interface_block, coupling, eigenvalues, mode_counts, interface_coords, modal_coords):
    block = interface_block[0]
    coup = coupling[0]
    coords = interface_coords[0]
    modal = modal_coords[0]
    width = coup.shape[1]
    levels = LEVELS
    index = jnp.arange(width, dtype=jnp.int32)
    mask = (index < mode_counts[0]).astype(jnp.float32)
    scaled = (coup.astype(jnp.float32) * (mask / eigenvalues[0])[None, :]).astype(jnp.bfloat16)
    columns = block
    schur = columns - lax.dot_general(
        scaled,
        lax.all_gather(coup, "panel", axis=0, tiled=True),
        (((1,), (1,)), ((), ())),
        preferred_element_type=jnp.float32,
    )
    merged = schur
    for level in range(levels):
        merged = merged + partner(merged, "leaf", level)
    owned = modal_reduce(jnp.dot(scaled, modal, preferred_element_type=jnp.float32), levels)
    columns = merged
    shapes = owned + jnp.dot(
        columns,
        lax.all_gather(coords, "panel", axis=0, tiled=True).astype(jnp.float32),
        precision=lax.Precision.HIGHEST,
    )
    return shapes[None]


def solution(mesh):
    placed = (
        P("leaf", "panel", None),
        P("leaf", "panel", None),
        P("leaf", None),
        P("leaf"),
        P("leaf", "panel", None),
        P("leaf", None, None),
    )
    return jax.shard_map(
        on_device, mesh=mesh, in_specs=placed, out_specs=P("leaf", "panel", None), check_vma=False
    )
```

profile of v0, /device:TPU:0, one launch (start us, length us, event | category | flops | bytes accessed | tf_op | source)
XLA Modules:
  0.0 233.8 jit_solution(16396193473058666457)
XLA Ops:
  6.5 0.0 copy-start
  6.5 0.0 all-gather.4.cloned.1.call-start
  7.3 8.9 %all-gather = bf16[1,2048,128]{2,1,0:T(8,128)(2,1)S(1)} all-gather(bf16[1,512,128]{2,1,0:T(8,128)(2,1)} %param.7), channel_id=2, replica_groups=mesh['leaf'=8,'panel'=4] {'panel'}, dimensions={1}, use_global_device_ids=true | all-gather | bytes 655360 | tf_op jit(solution)/shard_map/all_gather | solution.py:38
  16.1 0.7 fusion.15
  16.8 0.0 copy-start.3
  16.8 5.0 %bitcast_subtract_fusion = f32[512,2048]{1,0:T(8,128)} fusion(f32[1,512,2048]{2,1,0:T(8,128)} %param.6, bf16[1,2048,128]{2,1,0:T(8,128)(2,1)S(1)} %all-gather, bf16[1,512,128]{2,1,0:T(8,128)(2,1)} %param.7, f32[128]{0:T(128)S(1)} %fusion.15), kind=kOutput, calls=%fused_computation.2 | convolution fusion | flops 269680640 | bytes 9044480 | tf_op jit(solution)/shard_map/dot_general | solution.py:36
  21.8 1.5 collective-permute-start.2
  23.3 0.0 copy-done
  23.3 0.0 copy-done.3
  23.3 1.2 fusion.3
  24.6 0.0 copy-start.1
  24.6 2.4 %constant_dynamic-slice_fusion.1 = f32[512,2048]{1,0:T(8,128)} fusion(f32[512,4096]{1,0:T(8,128)S(1)} %fusion.3, s32[]{:T(128)S(6)} %select_n.13), kind=kLoop, calls=%fused_computation.19 | loop fusion | bytes 8388612 | tf_op jit(solution)/shard_map/dynamic_slice | solution.py:20
  27.0 2.1 copy-done.1
  29.1 1.6 collective-permute-start
  30.7 0.0 all-gather.4.cloned.1.call-update
  30.7 84.2 %collective-permute-done.2 = f32[512,2048]{1,0:T(8,128)} collective-permute-done((f32[512,2048]{1,0:T(8,128)}, f32[512,2048]{1,0:T(8,128)}, u32[]{:S(2)}, u32[]{:S(2)}) %collective-permute-start.2) | collective-permute-done | bytes 4194336 | tf_op jit(solution)/shard_map/ppermute | solution.py:10
  114.9 6.5 %add.33 = f32[512,2048]{1,0:T(8,128)} add(f32[512,2048]{1,0:T(8,128)} %bitcast_subtract_fusion, f32[512,2048]{1,0:T(8,128)} %collective-permute-done.2) | non-fusion elementwise | flops 1048576 | bytes 12582912 | tf_op jit(solution)/shard_map/add | solution.py:44
  121.4 1.6 collective-permute-start.3
  123.0 0.0 collective-permute-done
  123.0 4.2 %dynamic-slice_add_fusion = f32[512,2048]{1,0:T(8,128)S(1)} fusion(f32[512,2048]{1,0:T(8,128)} %collective-permute-done, f32[512,4096]{1,0:T(8,128)} %copy-done.1, s32[]{:T(128)S(6)} %select_n.12), kind=kLoop, calls=%fused_computation.4 | loop fusion | flops 1048576 | bytes 12582916 | tf_op jit(solution)/shard_map/add | solution.py:21
  127.3 0.0 copy-start.2
  127.3 1.9 copy-done.2
  129.2 0.1 constant_dynamic-slice_fusion
  129.3 1.6 collective-permute-start.1
  130.9 45.3 %collective-permute-done.1 = f32[512,1024]{1,0:T(8,128)} collective-permute-done((f32[512,1024]{1,0:T(8,128)S(1)}, f32[512,1024]{1,0:T(8,128)}, u32[]{:S(2)}, u32[]{:S(2)}) %collective-permute-start.1) | collective-permute-done | bytes 2097184 | tf_op jit(solution)/shard_map/ppermute | solution.py:10
  176.2 0.0 all-gather.4.cloned.1.call-done
  176.2 37.5 %collective-permute-done.3 = f32[512,2048]{1,0:T(8,128)} collective-permute-done((f32[512,2048]{1,0:T(8,128)}, f32[512,2048]{1,0:T(8,128)}, u32[]{:S(2)}, u32[]{:S(2)}) %collective-permute-start.3) | collective-permute-done | bytes 4194336 | tf_op jit(solution)/shard_map/ppermute | solution.py:10
  213.7 13.3 %add_bitcast_fusion = f32[1,512,1024]{2,1,0:T(8,128)} fusion(f32[512,1024]{1,0:T(8,128)} %collective-permute-done.1, f32[512,2048]{1,0:T(8,128)} %copy-done.2, s32[]{:T(128)S(6)} %select_n.14, bf16[1,2048,1024]{2,1,0:T(8,128)(2,1)} %all-gather.4.cloned.1.call-done, f32[512,2048]{1,0:T(8,128)} %add.33, f32[512,2048]{1,0:T(8,128)} %collective-permute-done.3), kind=kOutput, calls=%fused_computation.5 | convolution fusion | flops 12886999040 | bytes 18874372 | tf_op jit(solution)/shard_map/dot_general | solution.py:47
Async XLA Ops:
  6.5 16.8 %copy-start = (bf16[1,128,4096]{2,1,0:T(8,128)(2,1)S(1)}, bf16[1,128,4096]{2,1,0:T(8,128)(2,1)}, u32[]{:S(2)}) copy-start(bf16[1,128,4096]{2,1,0:T(8,128)(2,1)} %param.11) | copy-start | bytes 3145732
  6.5 169.7 %all-gather.4.cloned.1.call-start = ((), (), s32[]{:S(2)}) async-start(), calls=%async_computation | async-start | bytes 5242880 | tf_op jit(solution)/shard_map/all_gather | solution.py:49
  16.8 6.5 %copy-start.3 = (bf16[1,512,128]{2,1,0:T(8,128)(2,1)S(1)}, bf16[1,512,128]{2,1,0:T(8,128)(2,1)}, u32[]{:S(2)}) copy-start(bf16[1,512,128]{2,1,0:T(8,128)(2,1)} %param.7) | copy-start | bytes 393220
  21.8 93.1 %collective-permute-start.2 = (f32[512,2048]{1,0:T(8,128)}, f32[512,2048]{1,0:T(8,128)}, u32[]{:S(2)}, u32[]{:S(2)}) collective-permute-start(f32[512,2048]{1,0:T(8,128)} %bitcast_subtract_fusion), channel_id=1, source_target_pairs={{0,4},{4,0},{8,12},{12,8},{16,20},{20,16},{24,28},{28,24},{1,5},{5... | collective-permute-start | bytes 12582920 | tf_op jit(solution)/shard_map/ppermute | solution.py:10
  24.6 4.5 %copy-start.1 = (f32[512,4096]{1,0:T(8,128)}, f32[512,4096]{1,0:T(8,128)S(1)}, u32[]{:S(2)}) copy-start(f32[512,4096]{1,0:T(8,128)S(1)} %fusion.3) | copy-start | bytes 25165828
  29.1 93.9 %collective-permute-start = (f32[512,2048]{1,0:T(8,128)}, f32[512,2048]{1,0:T(8,128)}, u32[]{:S(2)}, u32[]{:S(2)}) collective-permute-start(f32[512,2048]{1,0:T(8,128)} %constant_dynamic-slice_fusion.1), channel_id=1, source_target_pairs={{0,8},{4,12},{8,0},{12,4},{16,24},{20,28},{24,16},{28,20},{1,9},{5... | collective-permute-start | bytes 12582920 | tf_op jit(solution)/shard_map/ppermute | solution.py:10
  121.4 92.3 %collective-permute-start.3 = (f32[512,2048]{1,0:T(8,128)}, f32[512,2048]{1,0:T(8,128)}, u32[]{:S(2)}, u32[]{:S(2)}) collective-permute-start(f32[512,2048]{1,0:T(8,128)} %add.33), channel_id=1, source_target_pairs={{0,8},{4,12},{8,0},{12,4},{16,24},{20,28},{24,16},{28,20},{1,9},{5... | collective-permute-start | bytes 12582920 | tf_op jit(solution)/shard_map/ppermute | solution.py:10
  127.3 1.9 copy-start.2
  129.3 46.9 %collective-permute-start.1 = (f32[512,1024]{1,0:T(8,128)S(1)}, f32[512,1024]{1,0:T(8,128)}, u32[]{:S(2)}, u32[]{:S(2)}) collective-permute-start(f32[512,1024]{1,0:T(8,128)S(1)} %constant_dynamic-slice_fusion), channel_id=1, source_target_pairs={{0,4},{4,0},{8,12},{12,8},{16,20},{20,16},{24,28},{28,24},{1,5},{5... | collective-permute-start | bytes 6291464 | tf_op jit(solution)/shard_map/ppermute | solution.py:10
Sparse Core Ops, SparseCore 0:
  30.8 33.3 all-gather.3
where the time goes:
time: 234 us
  waiting for transfers between devices  167 us (71%)
  matrix products  19.5 us (8%)
  between operations  14.2 us (6%)
  other arithmetic  11.4 us (5%)
  blocking collectives  8.86 us (4%)
  local copies, waits for them, and re-layouts  6.59 us (3%)
  starting transfers between devices  6.26 us (3%)
    ppermute x4, waiting for transfers between devices, partner(): lax.ppermute(value, axis, [(i, i ^ 1 << bit) for i in range(lax.axis_size...  167 us
    dot_general x1, matrix products, on_device(): jnp.dot(columns, lax.all_gather(coords, 'panel', axis=0, tiled=True).asty...  13.3 us
    all_gather x1, blocking collectives, on_device(): lax.all_gather(coup, 'panel', axis=0, tiled=True)  8.86 us
    add x1, other arithmetic, on_device(): merged = merged + partner(merged, 'leaf', level)  6.52 us
    ppermute x4, starting transfers between devices, partner(): lax.ppermute(value, axis, [(i, i ^ 1 << bit) for i in range(lax.axis_size...  6.26 us
    dot_general x1, matrix products, on_device(): lax.dot_general(scaled, lax.all_gather(coup, 'panel', axis=0, tiled=True)...  4.98 us
  transfers between devices with their start and end apart: 5, of which 3 were waited for; matrix products, arithmetic and copies ran while one was open for 6% of the time, Pallas kernels for 0%

commit v1 on v0

--- a/solution.py
+++ b/solution.py
@@ -2,6 +2,7 @@
 import jax.numpy as jnp
 from jax import lax
 from jax.sharding import PartitionSpec as P
+from jax.lax import all_to_all, axis_size
 
 LEVELS = 2
 
@@ -23,6 +24,16 @@
 
 
 def on_device(interface_block, coupling, eigenvalues, mode_counts, interface_coords, modal_coords):
+
+    def pieces_all_work(bus_axis, panel):
+        return all_to_all(
+            jnp.concatenate(axis_size(bus_axis) * [panel], axis=0),
+            tiled=True,
+            axis_name=bus_axis,
+            split_axis=0,
+            concat_axis=0,
+        )
+
     block = interface_block[0]
     coup = coupling[0]
     coords = interface_coords[0]
@@ -35,7 +46,7 @@
     columns = block
     schur = columns - lax.dot_general(
         scaled,
-        lax.all_gather(coup, "panel", axis=0, tiled=True),
+        pieces_all_work("panel", coup),
         (((1,), (1,)), ((), ())),
         preferred_element_type=jnp.float32,
     )

time: 234 us -> 238 us (1.017)
  blocking collectives: 8.86 us -> 0 us
  waiting for transfers between devices: 167 us -> 173 us
  starting transfers between devices: 6.26 us -> 11.4 us
    all_gather x1 -> x0, blocking collectives: 8.86 us -> none  [on_device(): lax.all_gather(coup, 'panel', axis=0, tiled=True)]
    all_to_all x0 -> x1, waiting for transfers between devices: none -> 7.5 us  [pieces_all_work(): all_to_all(jnp.concatenate(axis_size(bus_axis) * [panel], axis=0), tiled=...]
    all_to_all x0 -> x1, starting transfers between devices: none -> 4.24 us  [pieces_all_work(): all_to_all(jnp.concatenate(axis_size(bus_axis) * [panel], axis=0), tiled=...]
  transfers between devices with their start and end apart: 5 -> 6, of which waited for: 3 -> 4; matrix products, arithmetic and copies ran while one was open for 6% -> 6% of each run, Pallas kernels for 0% -> 0%
where the time goes in v1:
time: 238 us
  waiting for transfers between devices  173 us (73%)
  matrix products  19.5 us (8%)
  between operations  14.1 us (6%)
  other arithmetic  13.5 us (6%)
  starting transfers between devices  11.4 us (5%)
  local copies, waits for them, and re-layouts  6.55 us (3%)
    ppermute x4, waiting for transfers between devices, partner(): lax.ppermute(value, axis, [(i, i ^ 1 << bit) for i in range(lax.axis_size...  165 us
    dot_general x1, matrix products, on_device(): jnp.dot(columns, lax.all_gather(coords, 'panel', axis=0, tiled=True).asty...  13.3 us
    all_to_all x1, waiting for transfers between devices, pieces_all_work(): all_to_all(jnp.concatenate(axis_size(bus_axis) * [panel], axis=0), tiled=...  7.5 us
    ppermute x4, starting transfers between devices, partner(): lax.ppermute(value, axis, [(i, i ^ 1 << bit) for i in range(lax.axis_size...  7.17 us
    add x1, other arithmetic, on_device(): merged = merged + partner(merged, 'leaf', level)  6.51 us
    dot_general x1, matrix products, on_device(): lax.dot_general(scaled, pieces_all_work('panel', coup), (((1,), (1,)), ((...  4.96 us
  transfers between devices with their start and end apart: 6, of which 4 were waited for; matrix products, arithmetic and copies ran while one was open for 6% of the time, Pallas kernels for 0%

profile of v1, /device:TPU:0, one launch (start us, length us, event | category | flops | bytes accessed | tf_op | source)
XLA Modules:
  0.0 237.8 jit_solution(8588037617949100608)
XLA Ops:
  6.5 0.0 copy-start
  6.5 2.1 pad_maximum_fusion
  8.6 4.2 %all-to-all-start = ((bf16[4,512,128]{2,1,0:T(8,128)(2,1)}), bf16[4,512,128]{2,1,0:T(8,128)(2,1)S(1)}, u32[]{:S(2)}, u32[]{:S(2)}) async-start(bf16[4,512,128]{2,1,0:T(8,128)(2,1)} %bitcast.6), calls=%async_computation | async-start | bytes 1048576 | tf_op jit(solution)/shard_map/all_to_all | solution.py:29
  12.8 0.0 all-gather.3.cloned.1.call-start
  13.5 0.7 fusion.9
  14.1 7.5 %all-to-all-done = bf16[4,512,128]{2,1,0:T(8,128)(2,1)S(1)} async-done(((bf16[4,512,128]{2,1,0:T(8,128)(2,1)}), bf16[4,512,128]{2,1,0:T(8,128)(2,1)S(1)}, u32[]{:S(2)}, u32[]{:S(2)}) %all-to-all-start) | async-done | bytes 524320 | tf_op jit(solution)/shard_map/all_to_all | solution.py:29
  21.6 0.0 copy-start.3
  21.6 5.0 %bitcast_subtract_fusion = f32[512,2048]{1,0:T(8,128)} fusion(f32[1,512,2048]{2,1,0:T(8,128)} %param.6, bf16[2048,128]{1,0:T(8,128)(2,1)S(1)} %bitcast.24, bf16[1,512,128]{2,1,0:T(8,128)(2,1)} %param.7, f32[128]{0:T(128)S(1)} %fusion.9), kind=kOutput, calls=%fused_computation.2 | convolution fusion | flops 269680640 | bytes 9044480 | tf_op jit(solution)/shard_map/dot_general | solution.py:47
  26.6 2.2 collective-permute-start.2
  28.8 0.0 copy-done
  28.8 0.0 copy-done.3
  28.8 1.2 fusion.3
  30.1 0.0 copy-start.1
  30.1 2.4 %constant_dynamic-slice_fusion.1 = f32[512,2048]{1,0:T(8,128)} fusion(f32[512,4096]{1,0:T(8,128)S(1)} %fusion.3, s32[]{:T(128)S(6)} %select_n.13), kind=kLoop, calls=%fused_computation.13 | loop fusion | bytes 8388612 | tf_op jit(solution)/shard_map/dynamic_slice | solution.py:21
  32.5 2.1 copy-done.1
  34.6 1.6 collective-permute-start
  36.1 0.0 all-gather.3.cloned.1.call-update
  36.2 83.2 %collective-permute-done.2 = f32[512,2048]{1,0:T(8,128)} collective-permute-done((f32[512,2048]{1,0:T(8,128)}, f32[512,2048]{1,0:T(8,128)}, u32[]{:S(2)}, u32[]{:S(2)}) %collective-permute-start.2) | collective-permute-done | bytes 4194336 | tf_op jit(solution)/shard_map/ppermute | solution.py:11
  119.4 6.5 %add.33 = f32[512,2048]{1,0:T(8,128)} add(f32[512,2048]{1,0:T(8,128)} %bitcast_subtract_fusion, f32[512,2048]{1,0:T(8,128)} %collective-permute-done.2) | non-fusion elementwise | flops 1048576 | bytes 12582912 | tf_op jit(solution)/shard_map/add | solution.py:55
  125.9 1.8 collective-permute-start.3
  127.7 0.0 collective-permute-done
  127.7 4.2 %dynamic-slice_add_fusion = f32[512,2048]{1,0:T(8,128)S(1)} fusion(f32[512,2048]{1,0:T(8,128)} %collective-permute-done, f32[512,4096]{1,0:T(8,128)} %copy-done.1, s32[]{:T(128)S(6)} %select_n.12), kind=kLoop, calls=%fused_computation.4 | loop fusion | flops 1048576 | bytes 12582916 | tf_op jit(solution)/shard_map/add | solution.py:22
  131.9 0.0 copy-start.2
  132.0 1.9 copy-done.2
  133.9 0.1 constant_dynamic-slice_fusion
  134.0 1.6 collective-permute-start.1
  135.6 44.5 %collective-permute-done.1 = f32[512,1024]{1,0:T(8,128)} collective-permute-done((f32[512,1024]{1,0:T(8,128)S(1)}, f32[512,1024]{1,0:T(8,128)}, u32[]{:S(2)}, u32[]{:S(2)}) %collective-permute-start.1) | collective-permute-done | bytes 2097184 | tf_op jit(solution)/shard_map/ppermute | solution.py:11
  180.1 0.0 all-gather.3.cloned.1.call-done
  180.1 37.6 %collective-permute-done.3 = f32[512,2048]{1,0:T(8,128)} collective-permute-done((f32[512,2048]{1,0:T(8,128)}, f32[512,2048]{1,0:T(8,128)}, u32[]{:S(2)}, u32[]{:S(2)}) %collective-permute-start.3) | collective-permute-done | bytes 4194336 | tf_op jit(solution)/shard_map/ppermute | solution.py:11
  217.7 13.3 %add_bitcast_fusion = f32[1,512,1024]{2,1,0:T(8,128)} fusion(f32[512,1024]{1,0:T(8,128)} %collective-permute-done.1, f32[512,2048]{1,0:T(8,128)} %copy-done.2, s32[]{:T(128)S(6)} %select_n.14, bf16[1,2048,1024]{2,1,0:T(8,128)(2,1)} %all-gather.3.cloned.1.call-done, f32[512,2048]{1,0:T(8,128)} %add.33, f32[512,2048]{1,0:T(8,128)} %collective-permute-done.3), kind=kOutput, calls=%fused_computation.5 | convolution fusion | flops 12886999040 | bytes 18874372 | tf_op jit(solution)/shard_map/dot_general | solution.py:58
Async XLA Ops:
  6.5 22.3 %copy-start = (bf16[1,128,4096]{2,1,0:T(8,128)(2,1)S(1)}, bf16[1,128,4096]{2,1,0:T(8,128)(2,1)}, u32[]{:S(2)}) copy-start(bf16[1,128,4096]{2,1,0:T(8,128)(2,1)} %param.11) | copy-start | bytes 3145732
  8.6 13.1 %all-to-all-start = ((bf16[4,512,128]{2,1,0:T(8,128)(2,1)}), bf16[4,512,128]{2,1,0:T(8,128)(2,1)S(1)}, u32[]{:S(2)}, u32[]{:S(2)}) async-start(bf16[4,512,128]{2,1,0:T(8,128)(2,1)} %bitcast.6), calls=%async_computation | async-start | bytes 1048576 | tf_op jit(solution)/shard_map/all_to_all | solution.py:29
  12.8 167.3 %all-gather.3.cloned.1.call-start = ((), (), s32[]{:S(2)}) async-start(), calls=%async_computation.1 | async-start | bytes 5242880 | tf_op jit(solution)/shard_map/all_gather | solution.py:60
  21.6 7.2 %copy-start.3 = (bf16[1,512,128]{2,1,0:T(8,128)(2,1)S(1)}, bf16[1,512,128]{2,1,0:T(8,128)(2,1)}, u32[]{:S(2)}) copy-start(bf16[1,512,128]{2,1,0:T(8,128)(2,1)} %param.7) | copy-start | bytes 393220
  26.6 92.8 %collective-permute-start.2 = (f32[512,2048]{1,0:T(8,128)}, f32[512,2048]{1,0:T(8,128)}, u32[]{:S(2)}, u32[]{:S(2)}) collective-permute-start(f32[512,2048]{1,0:T(8,128)} %bitcast_subtract_fusion), channel_id=1, source_target_pairs={{0,4},{4,0},{8,12},{12,8},{16,20},{20,16},{24,28},{28,24},{1,5},{5... | collective-permute-start | bytes 12582920 | tf_op jit(solution)/shard_map/ppermute | solution.py:11
  30.1 4.5 %copy-start.1 = (f32[512,4096]{1,0:T(8,128)}, f32[512,4096]{1,0:T(8,128)S(1)}, u32[]{:S(2)}) copy-start(f32[512,4096]{1,0:T(8,128)S(1)} %fusion.3) | copy-start | bytes 25165828
  34.6 93.1 %collective-permute-start = (f32[512,2048]{1,0:T(8,128)}, f32[512,2048]{1,0:T(8,128)}, u32[]{:S(2)}, u32[]{:S(2)}) collective-permute-start(f32[512,2048]{1,0:T(8,128)} %constant_dynamic-slice_fusion.1), channel_id=1, source_target_pairs={{0,8},{4,12},{8,0},{12,4},{16,24},{20,28},{24,16},{28,20},{1,9},{5... | collective-permute-start | bytes 12582920 | tf_op jit(solution)/shard_map/ppermute | solution.py:11
  125.9 91.8 %collective-permute-start.3 = (f32[512,2048]{1,0:T(8,128)}, f32[512,2048]{1,0:T(8,128)}, u32[]{:S(2)}, u32[]{:S(2)}) collective-permute-start(f32[512,2048]{1,0:T(8,128)} %add.33), channel_id=1, source_target_pairs={{0,8},{4,12},{8,0},{12,4},{16,24},{20,28},{24,16},{28,20},{1,9},{5... | collective-permute-start | bytes 12582920 | tf_op jit(solution)/shard_map/ppermute | solution.py:11
  131.9 1.9 copy-start.2
  134.0 46.1 %collective-permute-start.1 = (f32[512,1024]{1,0:T(8,128)S(1)}, f32[512,1024]{1,0:T(8,128)}, u32[]{:S(2)}, u32[]{:S(2)}) collective-permute-start(f32[512,1024]{1,0:T(8,128)S(1)} %constant_dynamic-slice_fusion), channel_id=1, source_target_pairs={{0,4},{4,0},{8,12},{12,8},{16,20},{20,16},{24,28},{28,24},{1,5},{5... | collective-permute-start | bytes 6291464 | tf_op jit(solution)/shard_map/ppermute | solution.py:11
Sparse Core Ops, SparseCore 0:
  36.3 32.7 all-gather.2
